TPU v7x, 32 devices: a whole 2x2x4 slice. The times are simulated.
32 devices in a mesh: dp: 4 (over y, x), seq: 8 (over z, core).
Axes of the slice: x: 2, y: 2, z: 4, core: 2. Of those that a mesh axis runs over, the one named last changes fastest.
Arguments:
- asking_vectors_matrix: bfloat16 [4, 1024, 2048], P('dp', 'seq'), may hold values from -6 to 6
- matched_keys_matrix: bfloat16 [4, 1024, 2048], P('dp', 'seq'), may hold values from -6 to 6
- carried_vectors_matrix: bfloat16 [4, 1024, 2048], P('dp', 'seq'), may hold values from -6 to 6
- upstream_cotangent: bfloat16 [4, 1024, 2048], P('dp', 'seq'), may hold values from -6 to 6
- w_out: bfloat16 [2048, 2048], P('seq'), may hold values from -0.125 to 0.125
- panel_entry_offsets: int32 [4, 9], P('dp'), may hold values from 0 to 32, as said below
- rightward_panel_per_entry: int32 [4, 32], P('dp'), may hold values from 0 to 7, as said below
Outputs:
- layer_out: bfloat16 [4, 1024, 2048], P('dp', 'seq')
- q_grad: bfloat16 [4, 1024, 2048], P('dp', 'seq')
- k_grad: bfloat16 [4, 1024, 2048], P('dp', 'seq')
- v_grad: bfloat16 [4, 1024, 2048], P('dp', 'seq')
- w_out_grad: float32 [2048, 2048], P('seq')
Inputs may be any that keep to these rules, and one draw needn't show every extreme that they name: panel_entry_offsets[b, 0] is 0 and panel_entry_offsets never falls along a row; tile row r owns slots panel_entry_offsets[b, r] to panel_entry_offsets[b, r + 1] - 1, 1 to 8 of them, and its own tile r is among its blocks; in every subgraph one tile row holds all 8 tiles; panel_entry_offsets[b, 8], the used slots, lies between 16 and 32 and equals 32 for at least one subgraph. `rightward_panel_per_entry`: the slots of a tile row hold distinct column tiles in rising order; slots from panel_entry_offsets[b, 8] on hold arbitrary tile numbers that take no part.
All inputs are finite; a program needn't handle non-finite values.
Results may differ from a plain program's by a relative error of at most 0.034.
Values may be sent and summed in bfloat16 or wider, within the bound.
No kernel may reach another device: no remote copies, remote signals or barrier semaphores. Data moves between devices by JAX's collectives and lax.ppermute only.
A program may use at most 128 MiB of HBM per device.

v0:
```python
import math
import jax
import jax.numpy as jnp
from jax import lax
from jax.sharding import PartitionSpec as P

H = 16
HD = 128


def tile_mask(starts, columns, nodes):
    tile_count = starts.shape[0] - 1
    slot_count = columns.shape[0]
    tile_size = nodes // tile_count
    slot_index = jnp.arange(slot_count, dtype=jnp.int32)
    entry_row = jnp.sum((starts[1:][None, :] <= slot_index[:, None]).astype(jnp.int32), axis=1)
    tile_ids = jnp.arange(tile_count, dtype=jnp.int32)
    row_hot = (entry_row[:, None] == tile_ids[None, :]).astype(jnp.int32)
    col_hot = (columns[:, None] == tile_ids[None, :]).astype(jnp.int32)
    pairs = jnp.einsum("er,ec->rc", row_hot, col_hot) > 0
    full = jnp.broadcast_to(pairs[:, None, :, None], (tile_count, tile_size, tile_count, tile_size))
    return jnp.where(full.reshape(nodes, nodes), 0.0, -jnp.inf)


def attend(q, k, v, allowed):
    factor = 1.0 / math.sqrt(q.shape[-1])
    scores = jnp.dot(q, k.T, preferred_element_type=jnp.float32) * factor
    masked = scores + allowed
    row_max = jnp.max(masked, axis=1, keepdims=True)
    expd = jnp.exp(masked - row_max)
    row_total = jnp.sum(expd, axis=1, keepdims=True)
    weighted = jnp.dot(expd.astype(jnp.bfloat16), v, preferred_element_type=jnp.float32)
    attended = (weighted / row_total).astype(jnp.bfloat16)
    return (attended, expd, row_total)


def attend_back(q, k, v, g, attended, expd, row_total):
    factor = 1.0 / math.sqrt(q.shape[-1])
    prob = expd * (1.0 / row_total)
    prob_low = prob.astype(jnp.bfloat16)
    v_grad = jnp.dot(prob_low.T, g, preferred_element_type=jnp.float32)
    prob_grad = jnp.dot(g, v.T, preferred_element_type=jnp.float32)
    delta = jnp.sum(attended.astype(jnp.float32) * g.astype(jnp.float32), axis=1, keepdims=True)
    score_grad = (prob * (prob_grad - delta) * factor).astype(jnp.bfloat16)
    q_grad = jnp.dot(score_grad, k, preferred_element_type=jnp.float32)
    k_grad = jnp.dot(score_grad.T, q, preferred_element_type=jnp.float32)
    return (q_grad.astype(jnp.bfloat16), k_grad.astype(jnp.bfloat16), v_grad.astype(jnp.bfloat16))


def chip_layer_out(att_flat, w_out):
    n = lax.axis_size("seq")
    rows = att_flat.shape[0] // n
    chips = n // 2
    s = lax.axis_index("seq")
    core = s % 2
    z = s // 2
    sibling = [(i, i ^ 1) for i in range(n)]
    att_sib = lax.ppermute(att_flat, "seq", sibling)
    w_sib = lax.ppermute(w_out, "seq", sibling)

    def parity_rows(values):
        quads = values.reshape(chips, 2, rows, values.shape[1])
        return jnp.where(core == 0, quads[:, 0], quads[:, 1])

    att_chip = jnp.concatenate([parity_rows(att_flat), parity_rows(att_sib)], axis=2)
    w_chip = jnp.concatenate([w_out, w_sib], axis=0)
    chip_partial = lax.dot_general(
        att_chip, w_chip, (((2,), (0,)), ((), ())), preferred_element_type=jnp.float32
    )
    total = lax.dynamic_index_in_dim(chip_partial, z, 0, keepdims=False)
    sent = chip_partial.astype(jnp.bfloat16)
    for k in range(1, chips):
        pairs = [(i, (i // 2 + k) % chips * 2 + i % 2) for i in range(n)]
        piece = lax.dynamic_index_in_dim(sent, (z + k) % chips, 0, keepdims=False)
        total = total + lax.ppermute(piece, "seq", pairs).astype(jnp.float32)
    return total


def shards(
    asking_vectors_matrix,
    matched_keys_matrix,
    carried_vectors_matrix,
    upstream_cotangent,
    w_out,
    panel_entry_offsets,
    rightward_panel_per_entry,
):
    nodes_here = asking_vectors_matrix.shape[1]
    width = asking_vectors_matrix.shape[2]
    n_seq = lax.axis_size("seq")
    nodes = nodes_here * n_seq
    grad_here = upstream_cotangent[0]
    grad_full = lax.all_gather(grad_here, "seq", axis=0, tiled=True)
    groups = n_seq
    group_width = width // groups
    local_heads = group_width // HD

    def to_groups(values):
        return values.reshape(nodes_here, groups, group_width).transpose(1, 0, 2)

    stacked = jnp.stack(
        [
            to_groups(asking_vectors_matrix[0]),
            to_groups(matched_keys_matrix[0]),
            to_groups(carried_vectors_matrix[0]),
        ]
    )
    heads = lax.all_to_all(stacked, "seq", split_axis=1, concat_axis=1, tiled=True)
    heads = heads.reshape(3, nodes, group_width)
    allowed = tile_mask(panel_entry_offsets[0], rightward_panel_per_entry[0], nodes)

    def head_cols(values, h):
        return values[:, h * HD : (h + 1) * HD]

    fwd = [
        attend(head_cols(heads[0], h), head_cols(heads[1], h), head_cols(heads[2], h), allowed)
        for h in range(local_heads)
    ]
    att_flat = jnp.concatenate([f[0] for f in fwd], axis=1)
    layer_out = chip_layer_out(att_flat, w_out).astype(jnp.bfloat16)[None]
    g_flat = lax.dot_general(
        grad_full, w_out, (((1,), (1,)), ((), ())), preferred_element_type=jnp.float32
    ).astype(jnp.bfloat16)
    att_blocks = att_flat.reshape(n_seq, nodes_here, local_heads * HD)
    grad_blocks = grad_full.reshape(n_seq, nodes_here, width)
    terms = jnp.einsum(
        "bnf,bnk->bfk", att_blocks, grad_blocks, preferred_element_type=jnp.float32
    ).astype(jnp.bfloat16)
    w_rows = jnp.sum(terms.astype(jnp.float32), axis=0)
    w_rows = lax.psum(w_rows.astype(jnp.bfloat16), "dp").astype(jnp.float32)
    batch = asking_vectors_matrix.shape[0] * lax.axis_size("dp")
    w_out_grad = w_rows / batch
    bwd = [
        attend_back(
            head_cols(heads[0], h),
            head_cols(heads[1], h),
            head_cols(heads[2], h),
            head_cols(g_flat, h),
            fwd[h][0],
            fwd[h][1],
            fwd[h][2],
        )
        for h in range(local_heads)
    ]
    grads = jnp.stack(
        [
            jnp.concatenate([b[i] for b in bwd], axis=1).reshape(groups, nodes_here, group_width)
            for i in range(3)
        ]
    )
    back = lax.all_to_all(grads, "seq", split_axis=1, concat_axis=1, tiled=True)
    back = back.transpose(0, 2, 1, 3).reshape(3, 1, nodes_here, width)
    return (layer_out, back[0], back[1], back[2], w_out_grad)


def solution(mesh):
    return jax.shard_map(
        shards,
        mesh=mesh,
        in_specs=(
            P("dp", "seq", None),
            P("dp", "seq", None),
            P("dp", "seq", None),
            P("dp", "seq", None),
            P("seq", None),
            P("dp", None),
            P("dp", None),
        ),
        out_specs=(
            P("dp", "seq", None),
            P("dp", "seq", None),
            P("dp", "seq", None),
            P("dp", "seq", None),
            P("seq", None),
        ),
        check_vma=False,
    )
```

profile of v0, /device:TPU:10, one launch (start us, length us, event | category | flops | bytes accessed | tf_op | source)
XLA Modules:
  0.0 211.3 jit_solution(6985377320653367382)
XLA Ops:
  7.2 0.7 all-gather.3.cloned.1.call-update
  7.9 1.3 copy.72
  9.2 1.3 copy.73
  10.5 1.3 copy.74
  11.9 0.2 pad_maximum_fusion
  12.1 1.2 copy.75
  13.3 5.3 %all-to-all-start = ((bf16[3,8,128,256]{2,3,0,1:T(8,128)(2,1)}), bf16[3,8,128,256]{2,3,0,1:T(8,128)(2,1)S(1)}, u32[]{:S(2)}, u32[]{:S(2)}) async-start(bf16[3,8,128,256]{2,3,0,1:T(8,128)(2,1)} %copy.75), calls=%async_computation | async-start | bytes 3145728 | tf_op jit(solution)/shard_map/all_to_all | solution.py:108
  18.6 0.1 collective-permute-start.1
  18.9 0.1 convert_reduce_fusion.1
  19.0 0.3 fusion.38
  19.3 67.4 %all-to-all-done = bf16[3,8,128,256]{2,3,0,1:T(8,128)(2,1)S(1)} async-done(((bf16[3,8,128,256]{2,3,0,1:T(8,128)(2,1)}), bf16[3,8,128,256]{2,3,0,1:T(8,128)(2,1)S(1)}, u32[]{:S(2)}, u32[]{:S(2)}) %all-to-all-start) | async-done | bytes 1572896 | tf_op jit(solution)/shard_map/all_to_all | solution.py:108
  86.7 0.1 fusion.69
  86.8 0.2 copy.96
  87.1 0.2 copy.95
  87.3 0.2 copy.97
  87.5 0.3 broadcast_in_dim.14
  87.9 1.2 fusion.73
  89.1 0.6 fusion.2
  89.7 1.2 fusion.72
  90.9 0.1 copy-done
  91.1 0.6 fusion.4
  91.7 1.3 copy-done.2
  93.0 0.8 fusion.32
  93.9 3.9 %fusion.21 = bf16[1024,256]{0,1:T(8,128)(2,1)S(1)} fusion(bf16[256,2048]{1,0:T(8,128)(2,1)} %param.11, bf16[1,1024,2048]{2,1,0:T(8,128)(2,1)} %all-gather.3.cloned.1.call-done), kind=kOutput, calls=%fused_computation.32 | convolution fusion | flops 1074003968 | bytes 5767168 | tf_op jit(solution)/shard_map/dot_general | solution.py:121
  97.8 0.9 multiply_reduce_fusion.1
  98.7 1.2 multiply_convert_fusion.1
  99.9 0.5 convolution_convert_fusion.3
  100.4 0.8 convolution_convert_fusion.1
  101.2 0.8 copy-done.3
  102.1 1.2 multiply_convert_fusion
  103.3 0.5 convolution_convert_fusion.2
  103.8 0.8 convolution_convert_fusion
  104.6 1.1 fusion.31
  105.7 0.9 fusion.30
  106.7 1.0 fusion.67
  107.7 0.4 reshape.63
  108.1 0.1 copy.104
  108.4 0.1 copy.105
  108.6 0.1 copy.106
  108.8 1.4 pad_maximum_fusion.1
  110.1 6.9 %all-to-all-start.1 = ((bf16[3,8,128,256]{2,3,0,1:T(8,128)(2,1)}), bf16[3,8,128,256]{2,3,0,1:T(8,128)(2,1)S(1)}, u32[]{:S(2)}, u32[]{:S(2)}) async-start(bf16[3,8,128,256]{2,3,0,1:T(8,128)(2,1)} %pad_maximum_fusion.1), calls=%async_computation.1 | async-start | bytes 3145728 | tf_op jit(solution)/shard_map/all_to_all | solution.py:151
  117.0 1.5 fusion.70
  118.5 1.2 copy.98
  119.8 1.1 copy.99
  120.9 5.9 %convert_reduce_fusion = bf16[256,2048]{1,0:T(8,128)(2,1)} fusion(bf16[8,128,2048]{2,1,0:T(8,128)(2,1)} %bitcast.122, bf16[32,8,8,128]{3,2,1,0:T(8,128)(2,1)} %get-tuple-element.26), kind=kOutput, calls=%fused_computation | convolution fusion | flops 1081606144 | bytes 5767168 | tf_op jit(solution)/shard_map/bnf,bnk->bfk/dot_general | solution.py:126
  126.8 1.4 reshape.64
  128.2 0.7 fusion.71
  128.9 0.5 copy.100
  129.4 0.5 copy.101
  130.0 4.7 %fusion.74 = (bf16[4,128,2048]{2,1,0:T(8,128)(2,1)S(1)}, f32[4,128,2048]{2,1,0:T(8,128)}) fusion(bf16[256,2048]{1,0:T(8,128)(2,1)} %collective-permute-done.1, bf16[256,2048]{1,0:T(8,128)(2,1)} %param.11, bf16[4,128,256]{2,1,0:T(8,128)(2,1)S(1)} %get-tuple-element.39, bf16[4,128,256]{2,1,0:T(8,128)(2,1)S(1)} %get-tuple-element.40), kind=kOutput, calls=%fused_computation.99 | convolution fusion | flops 1080033280 | bytes 8912896 | tf_op jit(solution)/shard_map/dot_general | solution.py:67
  134.7 0.2 dynamic-slice_bitcast_fusion.2
  134.9 1.5 collective-permute-start.2
  136.4 1.0 collective-permute-start.3
  137.5 1.9 collective-permute-start.4
  139.4 41.1 %all-reduce.2.cloned.1.call-done = bf16[256,2048]{1,0:T(8,128)(2,1)} async-done(((bf16[256,2048]{1,0:T(8,128)(2,1)}), bf16[256,2048]{1,0:T(8,128)(2,1)}) %all-reduce.2.cloned.1.call-update) | async-done | bytes 1048592 | tf_op jit(solution)/shard_map/psum | solution.py:130
  180.4 2.8 %convert_multiply_fusion = f32[256,2048]{1,0:T(8,128)} fusion(bf16[256,2048]{1,0:T(8,128)(2,1)} %all-reduce.2.cloned.1.call-done), kind=kLoop, calls=%fused_computation.23 | loop fusion | flops 1048576 | bytes 3145728 | tf_op jit(solution)/shard_map/div | solution.py:132
  183.2 1.9 collective-permute-done.2
  185.1 11.2 %collective-permute-done.3 = bf16[128,2048]{1,0:T(8,128)(2,1)} collective-permute-done((bf16[128,2048]{1,0:T(8,128)(2,1)S(1)}, bf16[128,2048]{1,0:T(8,128)(2,1)}, u32[]{:S(2)}, u32[]{:S(2)}) %collective-permute-start.3) | collective-permute-done | bytes 524320 | tf_op jit(solution)/shard_map/ppermute | solution.py:75
  196.3 2.2 %collective-permute-done.4 = bf16[128,2048]{1,0:T(8,128)(2,1)} collective-permute-done((bf16[128,2048]{1,0:T(8,128)(2,1)S(1)}, bf16[128,2048]{1,0:T(8,128)(2,1)}, u32[]{:S(2)}, u32[]{:S(2)}) %collective-permute-start.4) | collective-permute-done | bytes 524320 | tf_op jit(solution)/shard_map/ppermute | solution.py:75
  198.5 2.8 %fusion.42 = bf16[1,128,2048]{2,1,0:T(8,128)(2,1)} fusion(bf16[128,2048]{1,0:T(8,128)(2,1)} %collective-permute-done.4, bf16[128,2048]{1,0:T(8,128)(2,1)} %collective-permute-done.3, bf16[128,2048]{1,0:T(8,128)(2,1)} %collective-permute-done.2, f32[4,128,2048]{2,1,0:T(8,128)} %get-tuple-element.37, s32[]{:T(128)S(6)} %select_n.72), kind=kLoop, calls=%fused_computation.49 | loop fusion | flops 1835008 | bytes 3145732 | tf_op jit(solution)/shard_map/broadcast_in_dim | solution.py:120
  201.3 0.1 fusion.68
  201.4 1.0 copy.90
  202.4 1.0 copy.91
  203.4 1.0 copy.92
  (28 shorter events, 0.7 us)
Async XLA Ops:
  7.2 86.7 %all-gather.3.cloned.1.call-start = ((), (), s32[]{:S(2)}) async-start(), calls=%async_computation.3 | async-start | bytes 4718592 | tf_op jit(solution)/shard_map/all_gather | solution.py:93
  11.9 6.9 %copy-start.4 = (s32[1,9]{1,0:T(1,128)S(1)}, s32[1,9]{1,0:T(1,128)}, u32[]{:S(2)}) copy-start(s32[1,9]{1,0:T(1,128)} %param.12) | copy-start | bytes 112
  11.9 7.1 %copy-start.5 = (s32[1,32]{1,0:T(1,128)S(1)}, s32[1,32]{1,0:T(1,128)}, u32[]{:S(2)}) copy-start(s32[1,32]{1,0:T(1,128)} %param.13) | copy-start | bytes 388
  13.3 73.4 %all-to-all-start = ((bf16[3,8,128,256]{2,3,0,1:T(8,128)(2,1)}), bf16[3,8,128,256]{2,3,0,1:T(8,128)(2,1)S(1)}, u32[]{:S(2)}, u32[]{:S(2)}) async-start(bf16[3,8,128,256]{2,3,0,1:T(8,128)(2,1)} %copy.75), calls=%async_computation | async-start | bytes 3145728 | tf_op jit(solution)/shard_map/all_to_all | solution.py:108
  18.6 111.3 %collective-permute-start.1 = (bf16[256,2048]{1,0:T(8,128)(2,1)}, bf16[256,2048]{1,0:T(8,128)(2,1)}, u32[]{:S(2)}, u32[]{:S(2)}) collective-permute-start(bf16[256,2048]{1,0:T(8,128)(2,1)} %param.11), channel_id=1, source_target_pairs={{0,1},{1,0},{2,3},{3,2},{4,5},{5,4},{6,7},{7,6},{8,9},{9,8},{10,11... | collective-permute-start | bytes 3145736 | tf_op jit(solution)/shard_map/ppermute | solution.py:59
  89.1 2.0 copy-start
  91.1 2.0 copy-start.2
  93.9 3.9 %copy-start.1 = (f32[1024,1024]{0,1:T(8,128)S(1)}, f32[1024,1024]{0,1:T(8,128)}, u32[]{:S(2)}) copy-start(f32[1024,1024]{0,1:T(8,128)} %copy-done) | copy-start | bytes 12582916
  99.9 2.2 %copy-start.3 = (f32[1024,1024]{0,1:T(8,128)S(1)}, f32[1024,1024]{0,1:T(8,128)}, u32[]{:S(2)}) copy-start(f32[1024,1024]{0,1:T(8,128)} %copy-done.2) | copy-start | bytes 12582916
  107.6 19.1 %collective-permute-start = (bf16[1024,256]{0,1:T(8,128)(2,1)S(1)}, bf16[1024,256]{0,1:T(8,128)(2,1)}, u32[]{:S(2)}, u32[]{:S(2)}) collective-permute-start(bf16[1024,256]{0,1:T(8,128)(2,1)S(1)} %get-tuple-element.27), channel_id=1, source_target_pairs={{0,1},{1,0},{2,3},{3,2},{4,5},{5,4},{6,7},{7,6},{8,9},{9,8},{10,11... | collective-permute-start | bytes 1572872 | tf_op jit(solution)/shard_map/ppermute | solution.py:58
  110.1 91.2 %all-to-all-start.1 = ((bf16[3,8,128,256]{2,3,0,1:T(8,128)(2,1)}), bf16[3,8,128,256]{2,3,0,1:T(8,128)(2,1)S(1)}, u32[]{:S(2)}, u32[]{:S(2)}) async-start(bf16[3,8,128,256]{2,3,0,1:T(8,128)(2,1)} %pad_maximum_fusion.1), calls=%async_computation.1 | async-start | bytes 3145728 | tf_op jit(solution)/shard_map/all_to_all | solution.py:151
  117.0 63.4 %all-reduce.2.cloned.1.call-start = ((), (), s32[]{:S(2)}) async-start(), calls=%async_computation.2 | async-start | bytes 2097152 | tf_op jit(solution)/shard_map/psum | solution.py:130
  134.9 50.2 %collective-permute-start.2 = (bf16[128,2048]{1,0:T(8,128)(2,1)S(1)}, bf16[128,2048]{1,0:T(8,128)(2,1)}, u32[]{:S(2)}, u32[]{:S(2)}) collective-permute-start(bf16[128,2048]{1,0:T(8,128)(2,1)S(1)} %get-tuple-element.17), channel_id=1, source_target_pairs={{0,2},{1,3},{2,4},{3,5},{4,6},{5,7},{6,0},{7,1},{8,10},{9,11},{10,... | collective-permute-start | bytes 1572872 | tf_op jit(solution)/shard_map/ppermute | solution.py:75
  136.4 59.8 %collective-permute-start.3 = (bf16[128,2048]{1,0:T(8,128)(2,1)S(1)}, bf16[128,2048]{1,0:T(8,128)(2,1)}, u32[]{:S(2)}, u32[]{:S(2)}) collective-permute-start(bf16[128,2048]{1,0:T(8,128)(2,1)S(1)} %get-tuple-element.19), channel_id=1, source_target_pairs={{0,4},{1,5},{2,6},{3,7},{4,0},{5,1},{6,2},{7,3},{8,12},{9,13},{10,... | collective-permute-start | bytes 1572872 | tf_op jit(solution)/shard_map/ppermute | solution.py:75
  137.5 61.0 %collective-permute-start.4 = (bf16[128,2048]{1,0:T(8,128)(2,1)S(1)}, bf16[128,2048]{1,0:T(8,128)(2,1)}, u32[]{:S(2)}, u32[]{:S(2)}) collective-permute-start(bf16[128,2048]{1,0:T(8,128)(2,1)S(1)} %get-tuple-element.18), channel_id=1, source_target_pairs={{0,6},{1,7},{2,0},{3,1},{4,2},{5,3},{6,4},{7,5},{8,14},{9,15},{10,... | collective-permute-start | bytes 1572872 | tf_op jit(solution)/shard_map/ppermute | solution.py:75
Sparse Core Ops, SparseCore 0:
  9.6 77.0 all-gather.2
  126.9 53.4 all-reduce.1
where the time goes:
time: 212 us; the launch traced here: 211 us
  waiting for transfers between devices  124 us (58%)
  matrix products  25.9 us (12%)
  local copies, waits for them, and re-layouts  19.9 us (9%)
  starting transfers between devices  17 us (8%)
  between operations  14.4 us (7%)
  other arithmetic  9.61 us (5%)
    all_to_all x1, waiting for transfers between devices, shards(): lax.all_to_all(stacked, 'seq', split_axis=1, concat_axis=1, tiled=True)  67.4 us
    psum x1, waiting for transfers between devices, shards(): w_rows = lax.psum(w_rows.astype(jnp.bfloat16), 'dp').astype(jnp.float32)  41.1 us
    ppermute x3, waiting for transfers between devices, chip_layer_out(): total = total + lax.ppermute(piece, 'seq', pairs).astype(jnp.float32)  15.3 us
    unnamed x28, local copies, waits for them, and re-layouts  13.5 us
    all_to_all x1, starting transfers between devices, shards(): back = lax.all_to_all(grads, 'seq', split_axis=1, concat_axis=1, tiled=True)  6.9 us
    dot_general x1, matrix products, shards(): jnp.einsum('bnf,bnk->bfk', att_blocks, grad_blocks, preferred_element_typ...  5.87 us
    all_to_all x1, starting transfers between devices, shards(): lax.all_to_all(stacked, 'seq', split_axis=1, concat_axis=1, tiled=True)  5.32 us
    dot_general x1, matrix products, chip_layer_out(): lax.dot_general(att_chip, w_chip, (((2,), (0,)), ((), ())), preferred_ele...  4.73 us
  transfers between devices with their start and end apart: 9, of which 5 were waited for; matrix products, arithmetic and copies ran while one was open for 24% of the time, Pallas kernels for 0%

commit v1 on v0

--- a/solution.py
+++ b/solution.py
@@ -148,7 +148,10 @@
             for i in range(3)
         ]
     )
-    back = lax.all_to_all(grads, "seq", split_axis=1, concat_axis=1, tiled=True)
+    back = jnp.concatenate(
+        lax.all_to_all(jnp.stack(jnp.split(grads, lax.axis_size("seq"), axis=1)), "seq", 0, 0),
+        axis=1,
+    )
     back = back.transpose(0, 2, 1, 3).reshape(3, 1, nodes_here, width)
     return (layer_out, back[0], back[1], back[2], w_out_grad)
 

time: 212 us -> 220 us (1.038)
  local copies, waits for them, and re-layouts: 19.9 us -> 26.4 us
    unnamed x28 -> x34, local copies, waits for them, and re-layouts: 13.5 us -> 18.1 us
  transfers between devices with their start and end apart: 9 -> 9, of which waited for: 5 -> 5; matrix products, arithmetic and copies ran while one was open for 24% -> 26% of each run, Pallas kernels for 0% -> 0%
where the time goes in v1:
time: 220 us; the launch traced here: 219 us
  waiting for transfers between devices  124 us (56%)
  matrix products  27.4 us (12%)
  local copies, waits for them, and re-layouts  26.4 us (12%)
  starting transfers between devices  17 us (8%)
  between operations  14.4 us (7%)
  other arithmetic  9.38 us (4%)
    all_to_all x1, waiting for transfers between devices, shards(): lax.all_to_all(stacked, 'seq', split_axis=1, concat_axis=1, tiled=True)  67.4 us
    psum x1, waiting for transfers between devices, shards(): w_rows = lax.psum(w_rows.astype(jnp.bfloat16), 'dp').astype(jnp.float32)  41 us
    unnamed x34, local copies, waits for them, and re-layouts  18.1 us
    ppermute x3, waiting for transfers between devices, chip_layer_out(): total = total + lax.ppermute(piece, 'seq', pairs).astype(jnp.float32)  15.3 us
    all_to_all x1, starting transfers between devices, shards(): lax.all_to_all(jnp.stack(jnp.split(grads, lax.axis_size('seq'), axis=1)),...  6.91 us
    dot_general x1, matrix products, shards(): jnp.einsum('bnf,bnk->bfk', att_blocks, grad_blocks, preferred_element_typ...  5.87 us
    all_to_all x1, starting transfers between devices, shards(): lax.all_to_all(stacked, 'seq', split_axis=1, concat_axis=1, tiled=True)  5.32 us
    dot_general x1, matrix products, chip_layer_out(): lax.dot_general(att_chip, w_chip, (((2,), (0,)), ((), ())), preferred_ele...  4.75 us
  transfers between devices with their start and end apart: 9, of which 5 were waited for; matrix products, arithmetic and copies ran while one was open for 26% of the time, Pallas kernels for 0%

profile of v1, /device:TPU:10, one launch (start us, length us, event | category | flops | bytes accessed | tf_op | source)
XLA Modules:
  0.0 219.0 jit_solution(15903925227728876794)
XLA Ops:
  7.2 0.7 all-gather.3.cloned.1.call-update
  7.9 1.3 copy.88
  9.2 1.3 copy.89
  10.5 1.3 copy.90
  12.1 1.2 copy.91
  13.3 5.3 %all-to-all-start = ((bf16[3,8,128,256]{2,3,0,1:T(8,128)(2,1)}), bf16[3,8,128,256]{2,3,0,1:T(8,128)(2,1)S(1)}, u32[]{:S(2)}, u32[]{:S(2)}) async-start(bf16[3,8,128,256]{2,3,0,1:T(8,128)(2,1)} %copy.91), calls=%async_computation | async-start | bytes 3145728 | tf_op jit(solution)/shard_map/all_to_all | solution.py:108
  19.0 0.3 fusion.38
  19.3 67.4 %all-to-all-done = bf16[3,8,128,256]{2,3,0,1:T(8,128)(2,1)S(1)} async-done(((bf16[3,8,128,256]{2,3,0,1:T(8,128)(2,1)}), bf16[3,8,128,256]{2,3,0,1:T(8,128)(2,1)S(1)}, u32[]{:S(2)}, u32[]{:S(2)}) %all-to-all-start) | async-done | bytes 1572896 | tf_op jit(solution)/shard_map/all_to_all | solution.py:108
  86.8 0.2 copy.118
  87.1 0.2 copy.117
  87.5 0.3 broadcast_in_dim.14
  87.9 1.2 fusion.81
  89.1 0.6 fusion.2
  89.7 1.2 fusion.80
  91.1 0.6 fusion.4
  91.7 1.3 copy-done.2
  93.0 0.8 fusion.32
  93.9 3.9 %fusion.21 = bf16[1024,256]{0,1:T(8,128)(2,1)S(1)} fusion(bf16[256,2048]{1,0:T(8,128)(2,1)} %param.11, bf16[1,1024,2048]{2,1,0:T(8,128)(2,1)} %all-gather.3.cloned.1.call-done), kind=kOutput, calls=%fused_computation.32 | convolution fusion | flops 1074003968 | bytes 5767168 | tf_op jit(solution)/shard_map/dot_general | solution.py:121
  97.8 0.9 multiply_reduce_fusion.1
  98.7 1.2 multiply_convert_fusion.1
  99.9 0.5 convolution_convert_fusion.3
  100.4 0.8 convolution_convert_fusion.1
  101.3 0.8 copy-done.3
  102.1 1.2 multiply_convert_fusion
  103.3 1.2 convolution_convert_fusion.2
  104.5 0.8 convolution_convert_fusion
  105.3 1.1 fusion.31
  106.5 1.6 fusion.30
  108.1 1.0 fusion.75
  109.2 0.4 reshape.69
  110.0 1.0 pad_maximum_fusion.5
  111.4 0.7 fusion.71
  112.1 0.7 fusion.70
  112.8 0.7 fusion.69
  113.5 0.7 fusion.68
  114.2 0.7 fusion.67
  114.9 0.7 fusion.66
  115.6 0.7 fusion.65
  116.3 0.7 fusion.64
  117.0 6.9 %all-to-all-start.1 = ((bf16[8,3,1,128,256]{4,3,1,2,0:T(8,128)(2,1)}), bf16[8,3,1,128,256]{4,3,1,2,0:T(8,128)(2,1)S(1)}, u32[]{:S(2)}, u32[]{:S(2)}) async-start(bf16[8,3,1,128,256]{4,3,1,2,0:T(8,128)(2,1)} %fusion.64), calls=%async_computation.1 | async-start | bytes 3145728 | tf_op jit(solution)/shard_map/all_to_all | solution.py:152
  123.9 1.5 fusion.78
  125.4 1.2 copy.120
  126.7 1.1 copy.121
  127.8 5.9 %convert_reduce_fusion = bf16[256,2048]{1,0:T(8,128)(2,1)} fusion(bf16[8,128,2048]{2,1,0:T(8,128)(2,1)} %bitcast.143, bf16[32,8,8,128]{3,2,1,0:T(8,128)(2,1)} %get-tuple-element.31), kind=kOutput, calls=%fused_computation | convolution fusion | flops 1081606144 | bytes 5767168 | tf_op jit(solution)/shard_map/bnf,bnk->bfk/dot_general | solution.py:126
  133.7 1.4 reshape.70
  135.1 0.7 fusion.79
  135.8 0.5 copy.122
  136.3 0.5 copy.123
  136.9 4.7 %fusion.82 = (bf16[4,128,2048]{2,1,0:T(8,128)(2,1)S(1)}, f32[4,128,2048]{2,1,0:T(8,128)}) fusion(bf16[256,2048]{1,0:T(8,128)(2,1)} %collective-permute-done.1, bf16[256,2048]{1,0:T(8,128)(2,1)} %param.11, bf16[4,128,256]{2,1,0:T(8,128)(2,1)S(1)} %get-tuple-element.44, bf16[4,128,256]{2,1,0:T(8,128)(2,1)S(1)} %get-tuple-element.45), kind=kOutput, calls=%fused_computation.115 | convolution fusion | flops 1080033280 | bytes 8912896 | tf_op jit(solution)/shard_map/dot_general | solution.py:67
  141.8 1.5 collective-permute-start.2
  143.3 1.0 collective-permute-start.3
  144.4 1.9 collective-permute-start.4
  146.3 41.0 %all-reduce.2.cloned.1.call-done = bf16[256,2048]{1,0:T(8,128)(2,1)} async-done(((bf16[256,2048]{1,0:T(8,128)(2,1)}), bf16[256,2048]{1,0:T(8,128)(2,1)}) %all-reduce.2.cloned.1.call-update) | async-done | bytes 1048592 | tf_op jit(solution)/shard_map/psum | solution.py:130
  187.3 2.8 %convert_multiply_fusion = f32[256,2048]{1,0:T(8,128)} fusion(bf16[256,2048]{1,0:T(8,128)(2,1)} %all-reduce.2.cloned.1.call-done), kind=kLoop, calls=%fused_computation.23 | loop fusion | flops 1048576 | bytes 3145728 | tf_op jit(solution)/shard_map/div | solution.py:132
  190.1 1.9 collective-permute-done.2
  192.0 11.2 %collective-permute-done.3 = bf16[128,2048]{1,0:T(8,128)(2,1)} collective-permute-done((bf16[128,2048]{1,0:T(8,128)(2,1)S(1)}, bf16[128,2048]{1,0:T(8,128)(2,1)}, u32[]{:S(2)}, u32[]{:S(2)}) %collective-permute-start.3) | collective-permute-done | bytes 524320 | tf_op jit(solution)/shard_map/ppermute | solution.py:75
  203.2 2.2 %collective-permute-done.4 = bf16[128,2048]{1,0:T(8,128)(2,1)} collective-permute-done((bf16[128,2048]{1,0:T(8,128)(2,1)S(1)}, bf16[128,2048]{1,0:T(8,128)(2,1)}, u32[]{:S(2)}, u32[]{:S(2)}) %collective-permute-start.4) | collective-permute-done | bytes 524320 | tf_op jit(solution)/shard_map/ppermute | solution.py:75
  205.4 2.8 %fusion.42 = bf16[1,128,2048]{2,1,0:T(8,128)(2,1)} fusion(bf16[128,2048]{1,0:T(8,128)(2,1)} %collective-permute-done.4, bf16[128,2048]{1,0:T(8,128)(2,1)} %collective-permute-done.3, bf16[128,2048]{1,0:T(8,128)(2,1)} %collective-permute-done.2, f32[4,128,2048]{2,1,0:T(8,128)} %get-tuple-element.42, s32[]{:T(128)S(6)} %select_n.72), kind=kLoop, calls=%fused_computation.49 | loop fusion | flops 1835008 | bytes 3145732 | tf_op jit(solution)/shard_map/broadcast_in_dim | solution.py:120
  208.3 0.3 copy.105
  208.6 1.0 copy.109
  209.6 0.3 copy.106
  209.9 1.0 copy.110
  210.9 0.3 copy.107
  211.2 1.0 copy.111
  (38 shorter events, 2.4 us)
Async XLA Ops:
  7.2 86.7 %all-gather.3.cloned.1.call-start = ((), (), s32[]{:S(2)}) async-start(), calls=%async_computation.3 | async-start | bytes 4718592 | tf_op jit(solution)/shard_map/all_gather | solution.py:93
  11.9 6.9 %copy-start.5 = (s32[1,9]{1,0:T(1,128)S(1)}, s32[1,9]{1,0:T(1,128)}, u32[]{:S(2)}) copy-start(s32[1,9]{1,0:T(1,128)} %param.12) | copy-start | bytes 112
  11.9 7.1 %copy-start.6 = (s32[1,32]{1,0:T(1,128)S(1)}, s32[1,32]{1,0:T(1,128)}, u32[]{:S(2)}) copy-start(s32[1,32]{1,0:T(1,128)} %param.13) | copy-start | bytes 388
  13.3 73.4 %all-to-all-start = ((bf16[3,8,128,256]{2,3,0,1:T(8,128)(2,1)}), bf16[3,8,128,256]{2,3,0,1:T(8,128)(2,1)S(1)}, u32[]{:S(2)}, u32[]{:S(2)}) async-start(bf16[3,8,128,256]{2,3,0,1:T(8,128)(2,1)} %copy.91), calls=%async_computation | async-start | bytes 3145728 | tf_op jit(solution)/shard_map/all_to_all | solution.py:108
  18.6 118.2 %collective-permute-start.1 = (bf16[256,2048]{1,0:T(8,128)(2,1)}, bf16[256,2048]{1,0:T(8,128)(2,1)}, u32[]{:S(2)}, u32[]{:S(2)}) collective-permute-start(bf16[256,2048]{1,0:T(8,128)(2,1)} %param.11), channel_id=1, source_target_pairs={{0,1},{1,0},{2,3},{3,2},{4,5},{5,4},{6,7},{7,6},{8,9},{9,8},{10,11... | collective-permute-start | bytes 3145736 | tf_op jit(solution)/shard_map/ppermute | solution.py:59
  89.1 2.0 copy-start
  91.0 2.0 copy-start.2
  93.9 3.9 %copy-start.1 = (f32[1024,1024]{0,1:T(8,128)S(1)}, f32[1024,1024]{0,1:T(8,128)}, u32[]{:S(2)}) copy-start(f32[1024,1024]{0,1:T(8,128)} %copy-done) | copy-start | bytes 12582916
  99.9 2.2 copy-start.3
  106.5 3.1 %copy-start.4 = (bf16[1024,128]{0,1:T(8,128)(2,1)S(1)}, bf16[1024,128]{0,1:T(8,128)(2,1)}, u32[]{:S(2)}) copy-start(bf16[1024,128]{0,1:T(8,128)(2,1)} %convolution_convert_fusion.2) | copy-start | bytes 786436
  109.1 24.6 %collective-permute-start = (bf16[1024,256]{0,1:T(8,128)(2,1)S(1)}, bf16[1024,256]{0,1:T(8,128)(2,1)}, u32[]{:S(2)}, u32[]{:S(2)}) collective-permute-start(bf16[1024,256]{0,1:T(8,128)(2,1)S(1)} %get-tuple-element.32), channel_id=1, source_target_pairs={{0,1},{1,0},{2,3},{3,2},{4,5},{5,4},{6,7},{7,6},{8,9},{9,8},{10,11... | collective-permute-start | bytes 1572872 | tf_op jit(solution)/shard_map/ppermute | solution.py:58
  117.0 91.2 %all-to-all-start.1 = ((bf16[8,3,1,128,256]{4,3,1,2,0:T(8,128)(2,1)}), bf16[8,3,1,128,256]{4,3,1,2,0:T(8,128)(2,1)S(1)}, u32[]{:S(2)}, u32[]{:S(2)}) async-start(bf16[8,3,1,128,256]{4,3,1,2,0:T(8,128)(2,1)} %fusion.64), calls=%async_computation.1 | async-start | bytes 3145728 | tf_op jit(solution)/shard_map/all_to_all | solution.py:152
  123.9 63.4 %all-reduce.2.cloned.1.call-start = ((), (), s32[]{:S(2)}) async-start(), calls=%async_computation.2 | async-start | bytes 2097152 | tf_op jit(solution)/shard_map/psum | solution.py:130
  141.8 50.2 %collective-permute-start.2 = (bf16[128,2048]{1,0:T(8,128)(2,1)S(1)}, bf16[128,2048]{1,0:T(8,128)(2,1)}, u32[]{:S(2)}, u32[]{:S(2)}) collective-permute-start(bf16[128,2048]{1,0:T(8,128)(2,1)S(1)} %get-tuple-element.22), channel_id=1, source_target_pairs={{0,2},{1,3},{2,4},{3,5},{4,6},{5,7},{6,0},{7,1},{8,10},{9,11},{10,... | collective-permute-start | bytes 1572872 | tf_op jit(solution)/shard_map/ppermute | solution.py:75
  143.3 59.8 %collective-permute-start.3 = (bf16[128,2048]{1,0:T(8,128)(2,1)S(1)}, bf16[128,2048]{1,0:T(8,128)(2,1)}, u32[]{:S(2)}, u32[]{:S(2)}) collective-permute-start(bf16[128,2048]{1,0:T(8,128)(2,1)S(1)} %get-tuple-element.24), channel_id=1, source_target_pairs={{0,4},{1,5},{2,6},{3,7},{4,0},{5,1},{6,2},{7,3},{8,12},{9,13},{10,... | collective-permute-start | bytes 1572872 | tf_op jit(solution)/shard_map/ppermute | solution.py:75
  144.4 61.0 %collective-permute-start.4 = (bf16[128,2048]{1,0:T(8,128)(2,1)S(1)}, bf16[128,2048]{1,0:T(8,128)(2,1)}, u32[]{:S(2)}, u32[]{:S(2)}) collective-permute-start(bf16[128,2048]{1,0:T(8,128)(2,1)S(1)} %get-tuple-element.23), channel_id=1, source_target_pairs={{0,6},{1,7},{2,0},{3,1},{4,2},{5,3},{6,4},{7,5},{8,14},{9,15},{10,... | collective-permute-start | bytes 1572872 | tf_op jit(solution)/shard_map/ppermute | solution.py:75
Sparse Core Ops, SparseCore 0:
  9.6 77.0 all-gather.2
  133.8 53.4 all-reduce.1
